TPU v7x, 256 devices: a whole 4x4x8 slice. The times are simulated.
256 devices in a mesh: gx: 16 (over z, core), gy: 16 (over y, x).
Axes of the slice: x: 4, y: 4, z: 8, core: 2. Of those that a mesh axis runs over, the one named last changes fastest.
Arguments:
- field: float32 [64, 4096, 128], P('gy', 'gx'), may hold values from -5 to 5
- courant: float32 [3, 64, 4096, 128], P(None, 'gy', 'gx'), may hold values from -2.5 to 2.5
- diffusion_number: float32 [64, 4096, 128], P('gy', 'gx'), may hold values from 65536 to 1310720
Outputs:
- solved: float32 [64, 4096, 128], P('gy', 'gx')
All inputs are finite; a program needn't handle non-finite values.
Results may differ from a plain program's by a relative error of at most 0.0013.
Values sent between devices are 32-bit elements; how exact they have to be, the bound alone decides.
No kernel may reach another device: no remote copies, remote signals or barrier semaphores. Data moves between devices by JAX's collectives and lax.ppermute only.
A program may use at most 64 MiB of HBM per device.

v0:
```python
import jax
import jax.numpy as jnp
from jax import lax
from jax.sharding import PartitionSpec as P


def padded_2(cells, sides, width, closed):
    for axis, dim in sides:
        count = lax.axis_size(axis)
        ends = count if closed else count - 1
        head = lax.slice_in_dim(cells, 0, width, axis=dim)
        tail = lax.slice_in_dim(cells, cells.shape[dim] - width, cells.shape[dim], axis=dim)
        cells = jnp.concatenate(
            [
                lax.ppermute(tail, axis, [(i, (i + 1) % count) for i in range(ends)]),
                cells,
                lax.ppermute(head, axis, [((i + 1) % count, i) for i in range(ends)]),
            ],
            axis=dim,
        )
    return cells


def difference_pair(padded, sweep_direction, length):
    shifted = [
        lax.slice_in_dim(padded, offset, offset + length, axis=sweep_direction)
        for offset in range(5)
    ]
    gradient = (8.0 * (shifted[3] - shifted[1]) - (shifted[4] - shifted[0])) / 12.0
    curvature = (
        16.0 * (shifted[3] + shifted[1]) - (shifted[4] + shifted[0]) - 30.0 * shifted[2]
    ) / 12.0
    return (gradient, curvature)


def build_rhs(field, courant, y_padded, x_padded):
    z_padded = jnp.concatenate([field[:, :, -2:], field, field[:, :, :2]], 2)
    grad_y, curve_y = difference_pair(y_padded, 0, field.shape[0])
    grad_x = difference_pair(x_padded, 1, field.shape[1])[0]
    grad_z, curve_z = difference_pair(z_padded, 2, field.shape[2])
    transport = courant[0] * grad_x + courant[1] * grad_y + courant[2] * grad_z
    return field - transport + 0.05 * (curve_y + curve_z) + 0.3 * field / (1.0 + field * field)


def rows_below(values, stride, fill, sweep_direction):
    length = values.shape[sweep_direction]
    filler = jnp.full_like(lax.slice_in_dim(values, 0, stride, axis=sweep_direction), fill)
    return jnp.concatenate(
        [filler, lax.slice_in_dim(values, 0, length - stride, axis=sweep_direction)],
        sweep_direction,
    )


def rows_above(values, stride, fill, sweep_direction):
    length = values.shape[sweep_direction]
    filler = jnp.full_like(
        lax.slice_in_dim(values, length - stride, length, axis=sweep_direction), fill
    )
    return jnp.concatenate(
        [lax.slice_in_dim(values, stride, length, axis=sweep_direction), filler], sweep_direction
    )


def combine_rows(own_rows, below_set, above_set):
    lower_band, main_diagonal, upper_band, right_hand_sides = own_rows
    low_sub, low_diag, low_super, low_rights = below_set
    high_sub, high_diag, high_super, high_rights = above_set
    factor_low = -lower_band / low_diag
    factor_high = -upper_band / high_diag
    new_sub = factor_low * low_sub
    new_super = factor_high * high_super
    new_diag = main_diagonal + factor_low * low_super + factor_high * high_sub
    new_rights = tuple(
        (
            value + factor_low * lower_value + factor_high * upper_value
            for value, lower_value, upper_value in zip(right_hand_sides, low_rights, high_rights)
        )
    )
    return (new_sub, new_diag, new_super, new_rights)


def parallel_cyclic_reduction(
    lower_band, main_diagonal, upper_band, right_hand_sides, sweep_direction
):
    length = main_diagonal.shape[sweep_direction]
    stride = 1
    while stride < length:
        below_set = (
            rows_below(lower_band, stride, 0.0, sweep_direction),
            rows_below(main_diagonal, stride, 1.0, sweep_direction),
            rows_below(upper_band, stride, 0.0, sweep_direction),
            tuple((rows_below(value, stride, 0.0, sweep_direction) for value in right_hand_sides)),
        )
        above_set = (
            rows_above(lower_band, stride, 0.0, sweep_direction),
            rows_above(main_diagonal, stride, 1.0, sweep_direction),
            rows_above(upper_band, stride, 0.0, sweep_direction),
            tuple((rows_above(value, stride, 0.0, sweep_direction) for value in right_hand_sides)),
        )
        lower_band, main_diagonal, upper_band, right_hand_sides = combine_rows(
            (lower_band, main_diagonal, upper_band, right_hand_sides), below_set, above_set
        )
        stride = stride * 2
    return tuple((value / main_diagonal for value in right_hand_sides))


def shards(field, courant, diffusion_number):
    y_padded = padded_2(field, (("gy", 0),), 2, True)
    x_padded = padded_2(field, (("gx", 1),), 2, False)
    rhs = build_rhs(field, courant, y_padded, x_padded)
    place = lax.axis_index("gx")
    device_count = lax.axis_size("gx")
    sub_full = -diffusion_number
    diag_full = 1.0 + 2.0 * diffusion_number
    super_full = -diffusion_number
    edge_zeros = jnp.zeros_like(rhs[:, 0:1])
    inner_zeros = jnp.zeros_like(rhs[:, 3:])
    sub_inner = jnp.concatenate([edge_zeros, sub_full[:, 2:-1]], 1)
    super_inner = jnp.concatenate([super_full[:, 1:-2], edge_zeros], 1)
    diag_inner = diag_full[:, 1:-1]
    first_unit = jnp.concatenate([-sub_full[:, 1:2], inner_zeros], 1)
    last_unit = jnp.concatenate([inner_zeros, -super_full[:, -2:-1]], 1)
    particular_solution, first_row_response, last_row_response = parallel_cyclic_reduction(
        sub_inner, diag_inner, super_inner, (rhs[:, 1:-1], first_unit, last_unit), 1
    )
    low_open = (place > 0).astype(jnp.float32)
    high_open = (place < device_count - 1).astype(jnp.float32)
    sub_first = sub_full[:, 0:1] * low_open
    diag_first = diag_full[:, 0:1] + super_full[:, 0:1] * first_row_response[:, 0:1]
    super_first = super_full[:, 0:1] * last_row_response[:, 0:1]
    right_first = rhs[:, 0:1] - super_full[:, 0:1] * particular_solution[:, 0:1]
    sub_last = sub_full[:, -1:] * first_row_response[:, -1:]
    diag_last = diag_full[:, -1:] + sub_full[:, -1:] * last_row_response[:, -1:]
    super_last = super_full[:, -1:] * high_open
    right_last = rhs[:, -1:] - sub_full[:, -1:] * particular_solution[:, -1:]
    reduced_sub = jnp.concatenate([sub_first, sub_last], 1)
    reduced_diag = jnp.concatenate([diag_first, diag_last], 1)
    reduced_super = jnp.concatenate([super_first, super_last], 1)
    reduced_right = jnp.concatenate([right_first, right_last], 1)
    gathered_lower_band, gathered_diagonal, gathered_upper_band, gathered_rhs = (
        lax.all_gather(reduced_sub, "gx", axis=1, tiled=True),
        lax.all_gather(reduced_diag, "gx", axis=1, tiled=True),
        lax.all_gather(reduced_super, "gx", axis=1, tiled=True),
        lax.all_gather(reduced_right, "gx", axis=1, tiled=True),
    )
    boundary_rows_gathered = parallel_cyclic_reduction(
        gathered_lower_band, gathered_diagonal, gathered_upper_band, (gathered_rhs,), 1
    )[0]
    ends = lax.dynamic_slice_in_dim(boundary_rows_gathered, 2 * place, 2, 1)
    interior = (
        particular_solution + first_row_response * ends[:, 0:1] + last_row_response * ends[:, 1:2]
    )
    return jnp.concatenate([ends[:, 0:1], interior, ends[:, 1:2]], 1)


def solution(mesh):
    in_specs = (P("gy", "gx", None), P(None, "gy", "gx", None), P("gy", "gx", None))
    out_specs = P("gy", "gx", None)
    return jax.shard_map(shards, mesh=mesh, in_specs=in_specs, out_specs=out_specs, check_vma=False)
```

profile of v0, /device:TPU:1, one launch (start us, length us, event | category | flops | bytes accessed | tf_op | source)
XLA Modules:
  0.0 117.3 jit_solution(6404665510396162908)
XLA Ops:
  0.0 1.4 %copy.19 = f32[4,256,128]{2,0,1:T(4,128)S(1)} copy(f32[4,256,128]{2,1,0:T(8,128)} %param.3) | data formatting | bytes 1048576 | tf_op args[0]
  1.4 4.9 %collective-permute-start.1 = (f32[4,2,128]{2,0,1:T(4,128)S(1)}, f32[4,2,128]{2,0,1:T(4,128)S(1)}, u32[]{:S(2)}, u32[]{:S(2)}) collective-permute-start(f32[4,2,128]{2,0,1:T(4,128)S(1)} %get-tuple-element.94), channel_id=1, source_target_pairs={{0,16},{16,32},{32,48},{48,64},{64,80},{80,96},{96,112},{112,128},... | collective-permute-start | bytes 12296 | tf_op jit(solution)/shard_map/ppermute | solution.py:15
  6.3 2.1 %collective-permute-start = (f32[4,2,128]{2,0,1:T(4,128)S(1)}, f32[4,2,128]{2,0,1:T(4,128)S(1)}, u32[]{:S(2)}, u32[]{:S(2)}) collective-permute-start(f32[4,2,128]{2,0,1:T(4,128)S(1)} %get-tuple-element.93), channel_id=1, source_target_pairs={{16,0},{32,16},{48,32},{64,48},{80,64},{96,80},{112,96},{128,112},... | collective-permute-start | bytes 12296 | tf_op jit(solution)/shard_map/ppermute | solution.py:17
  8.4 1.0 fusion.36
  9.4 4.9 %collective-permute-start.2 = (f32[2,256,128]{2,0,1:T(2,128)}, f32[2,256,128]{2,0,1:T(2,128)S(1)}, u32[]{:S(2)}, u32[]{:S(2)}) collective-permute-start(f32[2,256,128]{2,0,1:T(2,128)} %get-tuple-element.90), channel_id=1, source_target_pairs={{1,0},{2,1},{3,2},{4,3},{5,4},{6,5},{7,6},{8,7},{9,8},{10,9},{11,1... | collective-permute-start | bytes 786440 | tf_op jit(solution)/shard_map/ppermute | solution.py:17
  14.3 1.3 %fusion.37 = (f32[4,256,2]{2,0,1:T(4,128)}, f32[4,256,2]{2,0,1:T(4,128)}) fusion(f32[4,256,128]{2,0,1:T(4,128)S(1)} %copy.19), kind=kLoop, calls=%fused_computation.178 | loop fusion | bytes 32768 | tf_op jit(solution)/shard_map/slice | solution.py:37
  15.6 1.2 %fusion.32 = (f32[1,4,256,128]{3,2,1,0:T(8,128)}, f32[1,4,256,128]{3,2,1,0:T(8,128)}, f32[1,4,256,128]{3,2,1,0:T(8,128)}) fusion(f32[3,4,256,128]{3,2,1,0:T(8,128)S(1)} %copy-done.10), kind=kLoop, calls=%fused_computation.173 | loop fusion | bytes 3145728 | tf_op jit(solution)/shard_map/slice | solution.py:41
  16.9 0.5 copy_negate_fusion
  17.4 1.2 %fusion.33 = (f32[4,253,128]{2,0,1:T(4,128)S(1)}, f32[4,253,128]{2,0,1:T(4,128)S(1)}, f32[4,253,128]{2,0,1:T(4,128)}, f32[4,253,128]{2,0,1:T(4,128)}) fusion(f32[4,256,128]{2,0,1:T(4,128)S(1)} %get-tuple-element.85, f32[4,256,128]{2,0,1:T(4,128)S(1)} %get-tuple-element.86), kind=kLoop, calls=%fused_computation.174 | loop fusion | bytes 4145152 | tf_op jit(solution)/shard_map/slice | solution.py:119
  18.6 0.8 pad_slice_fusion.10
  19.5 1.1 pad_slice_fusion.8
  20.6 0.8 pad_slice_fusion.11
  21.5 0.4 constant_dynamic-update-slice_fusion.1
  22.0 2.4 %collective-permute-done.3 = f32[2,256,128]{2,0,1:T(2,128)} collective-permute-done((f32[2,256,128]{2,0,1:T(2,128)}, f32[2,256,128]{2,0,1:T(2,128)}, u32[]{:S(2)}, u32[]{:S(2)}) %collective-permute-start.3) | collective-permute-done | bytes 262176 | tf_op jit(solution)/shard_map/ppermute | solution.py:15
  24.4 4.7 %fusion.11 = f32[4,256,128]{2,0,1:T(4,128)S(1)} fusion(f32[4,256,128]{2,0,1:T(4,128)S(1)} %copy.19, f32[4,258,128]{2,0,1:T(4,128)S(1)} %get-tuple-element.96, f32[4,258,128]{2,0,1:T(4,128)S(1)} %constant_dynamic-update-slice_fusion, f32[1,4,256,128]{3,2,1,0:T(8,128)} %get-tuple-element.51, f32[1,4,256,128]{3,2,1,0:T(8,128)} %get-tuple-element.50, ...), kind=kLoop, calls=%fused_computation.28 | loop fusion | flops 6291456 | bytes 5259264 | tf_op jit(solution)/shard_map/add | solution.py:42
  29.2 0.1 fusion.35
  29.3 0.9 copy-done.4
  30.2 0.2 copy-done.5
  30.3 0.6 fusion.18
  30.9 0.3 fusion.17
  31.3 0.1 fusion.77
  31.4 0.1 fusion.78
  31.6 0.7 copy-done.6
  32.3 0.2 copy-done.7
  32.4 0.2 copy-done.8
  32.6 0.2 copy-done.9
  32.7 1.9 %multiply_add_fusion.26 = (f32[4,254,128]{2,0,1:T(4,128)S(1)}, f32[4,254,128]{2,0,1:T(4,128)S(1)}, f32[4,254,128]{2,0,1:T(4,128)S(1)}, f32[4,254,128]{2,0,1:T(4,...) fusion(f32[4,252,128]{2,0,1:T(4,128)S(1)} %get-tuple-element.178, ...), kind=kLoop, calls=%fused_computation.96 | loop fusion | flops 2340864 | bytes 9343992 | tf_op jit(solution)/shard_map/add | solution.py:75
  34.6 0.1 fusion.73
  34.8 0.1 fusion.75
  34.9 0.3 multiply_add_fusion.25
  35.2 0.1 fusion.74
  35.3 0.1 fusion.45
  35.5 0.1 fusion.52
  35.6 0.1 fusion.76
  35.8 1.3 %multiply_add_fusion.24 = (f32[4,254,128]{2,0,1:T(4,128)S(1)}, f32[4,254,128]{2,0,1:T(4,128)S(1)}, f32[4,254,128]{2,0,1:T(4,128)S(1)}, f32[4,254,128]{2,0,1:T(4,...) fusion(f32[4,250,128]{2,0,1:T(4,128)S(1)} %get-tuple-element.174, ...), kind=kLoop, calls=%fused_computation.90 | loop fusion | flops 2340864 | bytes 11386880 | tf_op jit(solution)/shard_map/add | solution.py:75
  37.0 0.1 fusion.69
  37.2 0.1 fusion.71
  37.3 0.3 multiply_add_fusion.23
  37.6 0.1 fusion.70
  37.7 0.1 fusion.44
  37.9 0.1 fusion.51
  38.0 0.1 fusion.72
  38.2 1.3 %multiply_add_fusion.22 = (f32[4,254,128]{2,0,1:T(4,128)S(1)}, f32[4,254,128]{2,0,1:T(4,128)S(1)}, f32[4,254,128]{2,0,1:T(4,128)S(1)}, f32[4,254,128]{2,0,1:T(4,...) fusion(f32[4,246,128]{2,0,1:T(4,128)S(1)} %get-tuple-element.166, ...), kind=kLoop, calls=%fused_computation.84 | loop fusion | flops 2340864 | bytes 11329536 | tf_op jit(solution)/shard_map/add | solution.py:75
  39.4 0.1 fusion.65
  39.6 0.1 fusion.67
  39.7 0.3 multiply_add_fusion.21
  40.1 0.1 fusion.43
  40.2 0.1 fusion.50
  40.4 0.1 fusion.68
  40.5 1.2 %multiply_add_fusion.20 = (f32[4,254,128]{2,0,1:T(4,128)S(1)}, f32[4,254,128]{2,0,1:T(4,128)S(1)}, f32[4,254,128]{2,0,1:T(4,128)S(1)}, f32[4,254,128]{2,0,1:T(4,...) fusion(f32[4,238,128]{2,0,1:T(4,128)S(1)} %get-tuple-element.158, ...), kind=kLoop, calls=%fused_computation.78 | loop fusion | flops 2340864 | bytes 11214848 | tf_op jit(solution)/shard_map/add | solution.py:75
  41.8 0.1 fusion.63
  42.0 0.3 multiply_add_fusion.19
  42.4 0.1 fusion.42
  42.8 1.1 multiply_add_fusion.18
  44.1 0.3 multiply_add_fusion.17
  44.8 1.1 multiply_add_fusion.16
  46.2 1.1 multiply_add_fusion.8
  47.5 0.5 add_divide_fusion.2
  48.0 20.7 %all_gather.12 = f32[4,32,128]{2,0,1:T(4,128)S(1)} all-gather(f32[4,2,128]{2,0,1:T(4,128)S(1)} %pad_maximum_fusion.5), channel_id=1, replica_groups=mesh['gx'=16,'gy'=16] {'gx'}, dimensions={1}, use_global_device_ids=true | all-gather | bytes 69632 | tf_op jit(solution)/shard_map/all_gather | solution.py:144
  68.8 0.7 add_divide_fusion.1
  69.5 15.0 %all_gather.15 = f32[4,32,128]{2,0,1:T(4,128)S(1)} all-gather(f32[4,2,128]{2,0,1:T(4,128)S(1)} %pad_maximum_fusion.8), channel_id=1, replica_groups=mesh['gx'=16,'gy'=16] {'gx'}, dimensions={1}, use_global_device_ids=true | all-gather | bytes 69632 | tf_op jit(solution)/shard_map/all_gather | solution.py:143
  84.5 15.7 %all_gather.14 = f32[4,32,128]{2,0,1:T(4,128)S(1)} all-gather(f32[4,2,128]{2,0,1:T(4,128)S(1)} %pad_maximum_fusion.7), channel_id=1, replica_groups=mesh['gx'=16,'gy'=16] {'gx'}, dimensions={1}, use_global_device_ids=true | all-gather | bytes 69632 | tf_op jit(solution)/shard_map/all_gather | solution.py:142
  100.3 14.9 %all_gather.13 = f32[4,32,128]{2,0,1:T(4,128)S(1)} all-gather(f32[4,2,128]{2,0,1:T(4,128)S(1)} %pad_maximum_fusion.6), channel_id=1, replica_groups=mesh['gx'=16,'gy'=16] {'gx'}, dimensions={1}, use_global_device_ids=true | all-gather | bytes 69632 | tf_op jit(solution)/shard_map/all_gather | solution.py:141
  116.5 0.8 copy.26
  (88 shorter events, 3.2 us)
Async XLA Ops:
  1.4 20.1 %collective-permute-start.1 = (f32[4,2,128]{2,0,1:T(4,128)S(1)}, f32[4,2,128]{2,0,1:T(4,128)S(1)}, u32[]{:S(2)}, u32[]{:S(2)}) collective-permute-start(f32[4,2,128]{2,0,1:T(4,128)S(1)} %get-tuple-element.94), channel_id=1, source_target_pairs={{0,16},{16,32},{32,48},{48,64},{64,80},{80,96},{96,112},{112,128},... | collective-permute-start | bytes 12296 | tf_op jit(solution)/shard_map/ppermute | solution.py:15
  6.3 9.3 %copy-start.10 = (f32[3,4,256,128]{3,2,1,0:T(8,128)S(1)}, f32[3,4,256,128]{3,2,1,0:T(8,128)}, u32[]{:S(2)}) copy-start(f32[3,4,256,128]{3,2,1,0:T(8,128)} %param.4) | copy-start | bytes 4718596
  6.3 15.6 %collective-permute-start = (f32[4,2,128]{2,0,1:T(4,128)S(1)}, f32[4,2,128]{2,0,1:T(4,128)S(1)}, u32[]{:S(2)}, u32[]{:S(2)}) collective-permute-start(f32[4,2,128]{2,0,1:T(4,128)S(1)} %get-tuple-element.93), channel_id=1, source_target_pairs={{16,0},{32,16},{48,32},{64,48},{80,64},{96,80},{112,96},{128,112},... | collective-permute-start | bytes 12296 | tf_op jit(solution)/shard_map/ppermute | solution.py:17
  9.4 12.6 %collective-permute-start.2 = (f32[2,256,128]{2,0,1:T(2,128)}, f32[2,256,128]{2,0,1:T(2,128)S(1)}, u32[]{:S(2)}, u32[]{:S(2)}) collective-permute-start(f32[2,256,128]{2,0,1:T(2,128)} %get-tuple-element.90), channel_id=1, source_target_pairs={{1,0},{2,1},{3,2},{4,3},{5,4},{6,5},{7,6},{8,7},{9,8},{10,9},{11,1... | collective-permute-start | bytes 786440 | tf_op jit(solution)/shard_map/ppermute | solution.py:17
  14.3 10.1 %collective-permute-start.3 = (f32[2,256,128]{2,0,1:T(2,128)}, f32[2,256,128]{2,0,1:T(2,128)}, u32[]{:S(2)}, u32[]{:S(2)}) collective-permute-start(f32[2,256,128]{2,0,1:T(2,128)} %get-tuple-element.89), channel_id=1, source_target_pairs={{0,1},{1,2},{2,3},{3,4},{4,5},{5,6},{6,7},{7,8},{8,9},{9,10},{10,1... | collective-permute-start | bytes 786440 | tf_op jit(solution)/shard_map/ppermute | solution.py:15
  15.6 1.3 %copy-start.11 = (f32[4,256,128]{2,1,0:T(8,128)S(1)}, f32[4,256,128]{2,1,0:T(8,128)}, u32[]{:S(2)}) copy-start(f32[4,256,128]{2,1,0:T(8,128)} %param.5) | copy-start | bytes 1572868
  18.6 2.9 %copy-start = (f32[4,256,128]{2,1,0:T(8,128)S(1)}, f32[4,256,128]{2,1,0:T(8,128)}, u32[]{:S(2)}) copy-start(f32[4,256,128]{2,1,0:T(8,128)} %param.3) | copy-start | bytes 1572868
  21.5 3.0 %copy-start.1 = (f32[4,256,2]{2,0,1:T(4,128)S(1)}, f32[4,256,2]{2,0,1:T(4,128)}, u32[]{:S(2)}) copy-start(f32[4,256,2]{2,0,1:T(4,128)} %get-tuple-element.91) | copy-start | bytes 24580
  21.5 3.0 %copy-start.2 = (f32[4,256,2]{2,0,1:T(4,128)S(1)}, f32[4,256,2]{2,0,1:T(4,128)}, u32[]{:S(2)}) copy-start(f32[4,256,2]{2,0,1:T(4,128)} %get-tuple-element.92) | copy-start | bytes 24580
  21.5 3.0 %copy-start.3 = (f32[1,4,256,128]{3,2,1,0:T(8,128)S(1)}, f32[1,4,256,128]{3,2,1,0:T(8,128)}, u32[]{:S(2)}) copy-start(f32[1,4,256,128]{3,2,1,0:T(8,128)} %get-tuple-element.49) | copy-start | bytes 1572868
  29.1 1.0 copy-start.4
  29.1 1.2 %copy-start.5 = (f32[4,253,128]{2,0,1:T(4,128)S(1)}, f32[4,253,128]{2,0,1:T(4,128)}, u32[]{:S(2)}) copy-start(f32[4,253,128]{2,0,1:T(4,128)} %get-tuple-element.225) | copy-start | bytes 1554436
  31.2 1.0 copy-start.6
  31.2 1.2 %copy-start.7 = (f32[4,253,128]{2,0,1:T(4,128)S(1)}, f32[4,253,128]{2,0,1:T(4,128)}, u32[]{:S(2)}) copy-start(f32[4,253,128]{2,0,1:T(4,128)} %get-tuple-element.226) | copy-start | bytes 1554436
  31.2 1.3 %copy-start.8 = (f32[4,253,128]{2,0,1:T(4,128)S(1)}, f32[4,253,128]{2,0,1:T(4,128)}, u32[]{:S(2)}) copy-start(f32[4,253,128]{2,0,1:T(4,128)} %get-tuple-element.227) | copy-start | bytes 1554436
  31.3 1.5 %copy-start.9 = (f32[4,253,128]{2,0,1:T(4,128)S(1)}, f32[4,253,128]{2,0,1:T(4,128)}, u32[]{:S(2)}) copy-start(f32[4,253,128]{2,0,1:T(4,128)} %pad_slice_fusion.11) | copy-start | bytes 1554436
where the time goes:
time: 118 us; the launch traced here: 117 us
  blocking collectives  66.3 us (56%)
  other arithmetic  18.4 us (16%)
  local copies, waits for them, and re-layouts  17.5 us (15%)
  starting transfers between devices  11.9 us (10%)
  waiting for transfers between devices  2.44 us (2%)
    all_gather x1, blocking collectives, shards(): lax.all_gather(reduced_right, 'gx', axis=1, tiled=True)  20.7 us
    all_gather x1, blocking collectives, shards(): lax.all_gather(reduced_diag, 'gx', axis=1, tiled=True)  15.7 us
    all_gather x1, blocking collectives, shards(): lax.all_gather(reduced_super, 'gx', axis=1, tiled=True)  15 us
    all_gather x1, blocking collectives, shards(): lax.all_gather(reduced_sub, 'gx', axis=1, tiled=True)  14.9 us
    add x11, other arithmetic, combine_rows(): value + factor_low * lower_value + factor_high * upper_value  9.81 us
    ppermute x2, starting transfers between devices, padded_2(): lax.ppermute(head, axis, [((i + 1) % count, i) for i in range(ends)])  6.98 us
    ppermute x2, starting transfers between devices, padded_2(): lax.ppermute(tail, axis, [(i, (i + 1) % count) for i in range(ends)])  4.93 us
    add x1, other arithmetic, build_rhs(): field - transport + 0.05 * (curve_y + curve_z)  4.7 us
  transfers between devices with their start and end apart: 4, of which 1 were waited for; matrix products, arithmetic and copies ran while one was open for 7% of the time, Pallas kernels for 0%

commit v1 on v0

--- a/solution.py
+++ b/solution.py
@@ -137,8 +137,16 @@
     reduced_diag = jnp.concatenate([diag_first, diag_last], 1)
     reduced_super = jnp.concatenate([super_first, super_last], 1)
     reduced_right = jnp.concatenate([right_first, right_last], 1)
+
+    def build_waves_on_mesh(arr_in, dim_k):
+        reached = jnp.concatenate(
+            lax.all_to_all(jnp.stack([arr_in] * lax.axis_size("gx"), axis=0), "gx", 0, 0),
+            axis=dim_k,
+        )
+        return reached
+
     gathered_lower_band, gathered_diagonal, gathered_upper_band, gathered_rhs = (
-        lax.all_gather(reduced_sub, "gx", axis=1, tiled=True),
+        build_waves_on_mesh(reduced_sub, 1),
         lax.all_gather(reduced_diag, "gx", axis=1, tiled=True),
         lax.all_gather(reduced_super, "gx", axis=1, tiled=True),
         lax.all_gather(reduced_right, "gx", axis=1, tiled=True),

time: 118 us -> 116 us (0.983)
  blocking collectives: 66.3 us -> 51.4 us
  waiting for transfers between devices: 2.44 us -> 10.2 us
  starting transfers between devices: 11.9 us -> 16.9 us
    all_gather x1 -> x0, blocking collectives: 14.9 us -> none  [shards(): lax.all_gather(reduced_sub, 'gx', axis=1, tiled=True)]
    all_to_all x0 -> x1, waiting for transfers between devices: none -> 7.75 us  [build_waves_on_mesh(): lax.all_to_all(jnp.stack([arr_in] * lax.axis_size('gx'), axis=0), 'gx', 0...]
    all_to_all x0 -> x1, starting transfers between devices: none -> 5.03 us  [build_waves_on_mesh(): lax.all_to_all(jnp.stack([arr_in] * lax.axis_size('gx'), axis=0), 'gx', 0...]
  transfers between devices with their start and end apart: 4 -> 5, of which waited for: 1 -> 2; matrix products, arithmetic and copies ran while one was open for 7% -> 7% of each run, Pallas kernels for 0% -> 0%
where the time goes in v1:
time: 116 us
  blocking collectives  51.4 us (44%)
  other arithmetic  18.4 us (16%)
  local copies, waits for them, and re-layouts  18.2 us (16%)
  starting transfers between devices  16.9 us (15%)
  waiting for transfers between devices  10.2 us (9%)
    all_gather x1, blocking collectives, shards(): lax.all_gather(reduced_right, 'gx', axis=1, tiled=True)  20.7 us
    all_gather x1, blocking collectives, shards(): lax.all_gather(reduced_diag, 'gx', axis=1, tiled=True)  15.7 us
    all_gather x1, blocking collectives, shards(): lax.all_gather(reduced_super, 'gx', axis=1, tiled=True)  15 us
    add x11, other arithmetic, combine_rows(): value + factor_low * lower_value + factor_high * upper_value  9.65 us
    all_to_all x1, waiting for transfers between devices, build_waves_on_mesh(): lax.all_to_all(jnp.stack([arr_in] * lax.axis_size('gx'), axis=0), 'gx', 0...  7.75 us
    ppermute x2, starting transfers between devices, padded_2(): lax.ppermute(head, axis, [((i + 1) % count, i) for i in range(ends)])  6.98 us
    all_to_all x1, starting transfers between devices, build_waves_on_mesh(): lax.all_to_all(jnp.stack([arr_in] * lax.axis_size('gx'), axis=0), 'gx', 0...  5.03 us
    ppermute x2, starting transfers between devices, padded_2(): lax.ppermute(tail, axis, [(i, (i + 1) % count) for i in range(ends)])  4.93 us
  transfers between devices with their start and end apart: 5, of which 2 were waited for; matrix products, arithmetic and copies ran while one was open for 7% of the time, Pallas kernels for 0%

profile of v1, /device:TPU:1, one launch (start us, length us, event | category | flops | bytes accessed | tf_op | source)
XLA Modules:
  0.0 115.9 jit_solution(6585161057471781886)
XLA Ops:
  0.0 1.4 %copy.19 = f32[4,256,128]{2,0,1:T(4,128)S(1)} copy(f32[4,256,128]{2,1,0:T(8,128)} %param.3) | data formatting | bytes 1048576 | tf_op args[0]
  1.4 4.9 %collective-permute-start.1 = (f32[4,2,128]{2,0,1:T(4,128)S(1)}, f32[4,2,128]{2,0,1:T(4,128)S(1)}, u32[]{:S(2)}, u32[]{:S(2)}) collective-permute-start(f32[4,2,128]{2,0,1:T(4,128)S(1)} %get-tuple-element.94), channel_id=1, source_target_pairs={{0,16},{16,32},{32,48},{48,64},{64,80},{80,96},{96,112},{112,128},... | collective-permute-start | bytes 12296 | tf_op jit(solution)/shard_map/ppermute | solution.py:15
  6.3 2.1 %collective-permute-start = (f32[4,2,128]{2,0,1:T(4,128)S(1)}, f32[4,2,128]{2,0,1:T(4,128)S(1)}, u32[]{:S(2)}, u32[]{:S(2)}) collective-permute-start(f32[4,2,128]{2,0,1:T(4,128)S(1)} %get-tuple-element.93), channel_id=1, source_target_pairs={{16,0},{32,16},{48,32},{64,48},{80,64},{96,80},{112,96},{128,112},... | collective-permute-start | bytes 12296 | tf_op jit(solution)/shard_map/ppermute | solution.py:17
  8.4 1.0 fusion.36
  9.4 4.9 %collective-permute-start.2 = (f32[2,256,128]{2,0,1:T(2,128)}, f32[2,256,128]{2,0,1:T(2,128)S(1)}, u32[]{:S(2)}, u32[]{:S(2)}) collective-permute-start(f32[2,256,128]{2,0,1:T(2,128)} %get-tuple-element.90), channel_id=1, source_target_pairs={{1,0},{2,1},{3,2},{4,3},{5,4},{6,5},{7,6},{8,7},{9,8},{10,9},{11,1... | collective-permute-start | bytes 786440 | tf_op jit(solution)/shard_map/ppermute | solution.py:17
  14.4 1.3 %fusion.37 = (f32[4,256,2]{2,0,1:T(4,128)}, f32[4,256,2]{2,0,1:T(4,128)}) fusion(f32[4,256,128]{2,0,1:T(4,128)S(1)} %copy.19), kind=kLoop, calls=%fused_computation.178 | loop fusion | bytes 32768 | tf_op jit(solution)/shard_map/slice | solution.py:37
  15.6 1.2 %fusion.32 = (f32[1,4,256,128]{3,2,1,0:T(8,128)}, f32[1,4,256,128]{3,2,1,0:T(8,128)}, f32[1,4,256,128]{3,2,1,0:T(8,128)}) fusion(f32[3,4,256,128]{3,2,1,0:T(8,128)S(1)} %copy-done.10), kind=kLoop, calls=%fused_computation.173 | loop fusion | bytes 3145728 | tf_op jit(solution)/shard_map/slice | solution.py:41
  16.9 0.5 copy_negate_fusion
  17.4 1.3 %fusion.33 = (f32[4,253,128]{2,0,1:T(4,128)S(1)}, f32[4,253,128]{2,0,1:T(4,128)S(1)}, f32[4,253,128]{2,0,1:T(4,128)}, f32[4,253,128]{2,0,1:T(4,128)}) fusion(f32[4,256,128]{2,0,1:T(4,128)S(1)} %get-tuple-element.85, f32[4,256,128]{2,0,1:T(4,128)S(1)} %get-tuple-element.86), kind=kLoop, calls=%fused_computation.174 | loop fusion | bytes 4145152 | tf_op jit(solution)/shard_map/slice | solution.py:119
  18.7 0.8 pad_slice_fusion.10
  19.5 1.1 pad_slice_fusion.8
  20.6 0.8 pad_slice_fusion.11
  21.5 0.4 constant_dynamic-update-slice_fusion.1
  22.0 2.4 %collective-permute-done.3 = f32[2,256,128]{2,0,1:T(2,128)} collective-permute-done((f32[2,256,128]{2,0,1:T(2,128)}, f32[2,256,128]{2,0,1:T(2,128)}, u32[]{:S(2)}, u32[]{:S(2)}) %collective-permute-start.3) | collective-permute-done | bytes 262176 | tf_op jit(solution)/shard_map/ppermute | solution.py:15
  24.4 4.7 %fusion.11 = f32[4,256,128]{2,0,1:T(4,128)S(1)} fusion(f32[4,256,128]{2,0,1:T(4,128)S(1)} %copy.19, f32[4,258,128]{2,0,1:T(4,128)S(1)} %get-tuple-element.96, f32[4,258,128]{2,0,1:T(4,128)S(1)} %constant_dynamic-update-slice_fusion, f32[1,4,256,128]{3,2,1,0:T(8,128)} %get-tuple-element.51, f32[1,4,256,128]{3,2,1,0:T(8,128)} %get-tuple-element.50, ...), kind=kLoop, calls=%fused_computation.28 | loop fusion | flops 6291456 | bytes 5259264 | tf_op jit(solution)/shard_map/add | solution.py:42
  29.2 0.1 fusion.35
  29.3 0.9 copy-done.4
  30.2 0.2 copy-done.5
  30.4 0.6 fusion.18
  31.0 0.3 fusion.17
  31.3 0.1 fusion.77
  31.4 0.1 fusion.78
  31.6 0.7 copy-done.6
  32.3 0.2 copy-done.7
  32.4 0.2 copy-done.8
  32.6 0.2 copy-done.9
  32.8 1.8 %multiply_add_fusion.26 = (f32[4,254,128]{2,0,1:T(4,128)S(1)}, f32[4,254,128]{2,0,1:T(4,128)S(1)}, f32[4,254,128]{2,0,1:T(4,128)S(1)}, f32[4,254,128]{2,0,1:T(4,...) fusion(f32[4,252,128]{2,0,1:T(4,128)S(1)} %get-tuple-element.178, ...), kind=kLoop, calls=%fused_computation.96 | loop fusion | flops 2340864 | bytes 9343992 | tf_op jit(solution)/shard_map/add | solution.py:75
  34.6 0.1 fusion.73
  34.7 0.1 fusion.75
  34.9 0.3 multiply_add_fusion.25
  35.2 0.1 fusion.74
  35.3 0.1 fusion.45
  35.4 0.1 fusion.52
  35.6 0.1 fusion.76
  35.7 1.3 %multiply_add_fusion.24 = (f32[4,254,128]{2,0,1:T(4,128)S(1)}, f32[4,254,128]{2,0,1:T(4,128)S(1)}, f32[4,254,128]{2,0,1:T(4,128)S(1)}, f32[4,254,128]{2,0,1:T(4,...) fusion(f32[4,250,128]{2,0,1:T(4,128)S(1)} %get-tuple-element.174, ...), kind=kLoop, calls=%fused_computation.90 | loop fusion | flops 2340864 | bytes 11386880 | tf_op jit(solution)/shard_map/add | solution.py:75
  37.0 0.1 fusion.69
  37.1 0.1 fusion.71
  37.3 0.3 multiply_add_fusion.23
  37.6 0.1 fusion.70
  37.7 0.1 fusion.44
  37.8 0.1 fusion.51
  38.0 0.1 fusion.72
  38.1 1.2 %multiply_add_fusion.22 = (f32[4,254,128]{2,0,1:T(4,128)S(1)}, f32[4,254,128]{2,0,1:T(4,128)S(1)}, f32[4,254,128]{2,0,1:T(4,128)S(1)}, f32[4,254,128]{2,0,1:T(4,...) fusion(f32[4,246,128]{2,0,1:T(4,128)S(1)} %get-tuple-element.166, ...), kind=kLoop, calls=%fused_computation.84 | loop fusion | flops 2340864 | bytes 11329536 | tf_op jit(solution)/shard_map/add | solution.py:75
  39.3 0.1 fusion.65
  39.5 0.1 fusion.67
  39.6 0.3 multiply_add_fusion.21
  40.0 0.1 fusion.43
  40.2 0.1 fusion.50
  40.5 1.2 %multiply_add_fusion.20 = (f32[4,254,128]{2,0,1:T(4,128)S(1)}, f32[4,254,128]{2,0,1:T(4,128)S(1)}, f32[4,254,128]{2,0,1:T(4,128)S(1)}, f32[4,254,128]{2,0,1:T(4,...) fusion(f32[4,238,128]{2,0,1:T(4,128)S(1)} %get-tuple-element.158, ...), kind=kLoop, calls=%fused_computation.78 | loop fusion | flops 2340864 | bytes 11214848 | tf_op jit(solution)/shard_map/add | solution.py:75
  41.9 0.3 multiply_add_fusion.19
  42.7 1.1 multiply_add_fusion.18
  44.0 0.3 multiply_add_fusion.17
  44.7 1.1 multiply_add_fusion.16
  46.2 1.0 multiply_add_fusion.8
  47.4 0.5 add_divide_fusion.2
  47.9 20.7 %all_gather.9 = f32[4,32,128]{2,0,1:T(4,128)S(1)} all-gather(f32[4,2,128]{2,0,1:T(4,128)S(1)} %pad_maximum_fusion.5), channel_id=1, replica_groups=mesh['gx'=16,'gy'=16] {'gx'}, dimensions={1}, use_global_device_ids=true | all-gather | bytes 69632 | tf_op jit(solution)/shard_map/all_gather | solution.py:152
  68.7 0.7 add_divide_fusion.1
  69.4 15.0 %all_gather.11 = f32[4,32,128]{2,0,1:T(4,128)S(1)} all-gather(f32[4,2,128]{2,0,1:T(4,128)S(1)} %pad_maximum_fusion.8), channel_id=1, replica_groups=mesh['gx'=16,'gy'=16] {'gx'}, dimensions={1}, use_global_device_ids=true | all-gather | bytes 69632 | tf_op jit(solution)/shard_map/all_gather | solution.py:151
  84.4 15.7 %all_gather.10 = f32[4,32,128]{2,0,1:T(4,128)S(1)} all-gather(f32[4,2,128]{2,0,1:T(4,128)S(1)} %pad_maximum_fusion.7), channel_id=1, replica_groups=mesh['gx'=16,'gy'=16] {'gx'}, dimensions={1}, use_global_device_ids=true | all-gather | bytes 69632 | tf_op jit(solution)/shard_map/all_gather | solution.py:150
  100.2 0.6 stack.2
  100.8 5.0 %all-to-all-start = ((f32[16,4,2,128]{3,2,1,0:T(2,128)}), f32[16,4,2,128]{3,2,1,0:T(2,128)S(1)}, u32[]{:S(2)}, u32[]{:S(2)}) async-start(f32[16,4,2,128]{3,2,1,0:T(2,128)} %stack.2), calls=%async_computation | async-start | bytes 131072 | tf_op jit(solution)/shard_map/all_to_all | solution.py:143
  105.9 7.8 %all-to-all-done = f32[16,4,2,128]{3,2,1,0:T(2,128)S(1)} async-done(((f32[16,4,2,128]{3,2,1,0:T(2,128)}), f32[16,4,2,128]{3,2,1,0:T(2,128)S(1)}, u32[]{:S(2)}, u32[]{:S(2)}) %all-to-all-start) | async-done | bytes 65568 | tf_op jit(solution)/shard_map/all_to_all | solution.py:143
  113.8 0.1 multiply_add_fusion.32
  115.0 0.8 copy.28
  (92 shorter events, 3.5 us)
Async XLA Ops:
  1.4 20.1 %collective-permute-start.1 = (f32[4,2,128]{2,0,1:T(4,128)S(1)}, f32[4,2,128]{2,0,1:T(4,128)S(1)}, u32[]{:S(2)}, u32[]{:S(2)}) collective-permute-start(f32[4,2,128]{2,0,1:T(4,128)S(1)} %get-tuple-element.94), channel_id=1, source_target_pairs={{0,16},{16,32},{32,48},{48,64},{64,80},{80,96},{96,112},{112,128},... | collective-permute-start | bytes 12296 | tf_op jit(solution)/shard_map/ppermute | solution.py:15
  6.3 9.3 %copy-start.10 = (f32[3,4,256,128]{3,2,1,0:T(8,128)S(1)}, f32[3,4,256,128]{3,2,1,0:T(8,128)}, u32[]{:S(2)}) copy-start(f32[3,4,256,128]{3,2,1,0:T(8,128)} %param.4) | copy-start | bytes 4718596
  6.3 15.6 %collective-permute-start = (f32[4,2,128]{2,0,1:T(4,128)S(1)}, f32[4,2,128]{2,0,1:T(4,128)S(1)}, u32[]{:S(2)}, u32[]{:S(2)}) collective-permute-start(f32[4,2,128]{2,0,1:T(4,128)S(1)} %get-tuple-element.93), channel_id=1, source_target_pairs={{16,0},{32,16},{48,32},{64,48},{80,64},{96,80},{112,96},{128,112},... | collective-permute-start | bytes 12296 | tf_op jit(solution)/shard_map/ppermute | solution.py:17
  9.4 12.6 %collective-permute-start.2 = (f32[2,256,128]{2,0,1:T(2,128)}, f32[2,256,128]{2,0,1:T(2,128)S(1)}, u32[]{:S(2)}, u32[]{:S(2)}) collective-permute-start(f32[2,256,128]{2,0,1:T(2,128)} %get-tuple-element.90), channel_id=1, source_target_pairs={{1,0},{2,1},{3,2},{4,3},{5,4},{6,5},{7,6},{8,7},{9,8},{10,9},{11,1... | collective-permute-start | bytes 786440 | tf_op jit(solution)/shard_map/ppermute | solution.py:17
  14.3 10.1 %collective-permute-start.3 = (f32[2,256,128]{2,0,1:T(2,128)}, f32[2,256,128]{2,0,1:T(2,128)}, u32[]{:S(2)}, u32[]{:S(2)}) collective-permute-start(f32[2,256,128]{2,0,1:T(2,128)} %get-tuple-element.89), channel_id=1, source_target_pairs={{0,1},{1,2},{2,3},{3,4},{4,5},{5,6},{6,7},{7,8},{8,9},{9,10},{10,1... | collective-permute-start | bytes 786440 | tf_op jit(solution)/shard_map/ppermute | solution.py:15
  15.6 1.3 %copy-start.11 = (f32[4,256,128]{2,1,0:T(8,128)S(1)}, f32[4,256,128]{2,1,0:T(8,128)}, u32[]{:S(2)}) copy-start(f32[4,256,128]{2,1,0:T(8,128)} %param.5) | copy-start | bytes 1572868
  18.7 2.9 %copy-start = (f32[4,256,128]{2,1,0:T(8,128)S(1)}, f32[4,256,128]{2,1,0:T(8,128)}, u32[]{:S(2)}) copy-start(f32[4,256,128]{2,1,0:T(8,128)} %param.3) | copy-start | bytes 1572868
  21.5 3.0 %copy-start.1 = (f32[4,256,2]{2,0,1:T(4,128)S(1)}, f32[4,256,2]{2,0,1:T(4,128)}, u32[]{:S(2)}) copy-start(f32[4,256,2]{2,0,1:T(4,128)} %get-tuple-element.91) | copy-start | bytes 24580
  21.5 3.0 %copy-start.2 = (f32[4,256,2]{2,0,1:T(4,128)S(1)}, f32[4,256,2]{2,0,1:T(4,128)}, u32[]{:S(2)}) copy-start(f32[4,256,2]{2,0,1:T(4,128)} %get-tuple-element.92) | copy-start | bytes 24580
  21.5 3.0 %copy-start.3 = (f32[1,4,256,128]{3,2,1,0:T(8,128)S(1)}, f32[1,4,256,128]{3,2,1,0:T(8,128)}, u32[]{:S(2)}) copy-start(f32[1,4,256,128]{3,2,1,0:T(8,128)} %get-tuple-element.49) | copy-start | bytes 1572868
  29.2 1.0 copy-start.4
  29.2 1.2 %copy-start.5 = (f32[4,253,128]{2,0,1:T(4,128)S(1)}, f32[4,253,128]{2,0,1:T(4,128)}, u32[]{:S(2)}) copy-start(f32[4,253,128]{2,0,1:T(4,128)} %get-tuple-element.225) | copy-start | bytes 1554436
  31.2 1.0 copy-start.6
  31.3 1.2 %copy-start.7 = (f32[4,253,128]{2,0,1:T(4,128)S(1)}, f32[4,253,128]{2,0,1:T(4,128)}, u32[]{:S(2)}) copy-start(f32[4,253,128]{2,0,1:T(4,128)} %get-tuple-element.226) | copy-start | bytes 1554436
  31.3 1.3 %copy-start.8 = (f32[4,253,128]{2,0,1:T(4,128)S(1)}, f32[4,253,128]{2,0,1:T(4,128)}, u32[]{:S(2)}) copy-start(f32[4,253,128]{2,0,1:T(4,128)} %get-tuple-element.227) | copy-start | bytes 1554436
  31.3 1.5 %copy-start.9 = (f32[4,253,128]{2,0,1:T(4,128)S(1)}, f32[4,253,128]{2,0,1:T(4,128)}, u32[]{:S(2)}) copy-start(f32[4,253,128]{2,0,1:T(4,128)} %pad_slice_fusion.11) | copy-start | bytes 1554436
  100.8 12.8 %all-to-all-start = ((f32[16,4,2,128]{3,2,1,0:T(2,128)}), f32[16,4,2,128]{3,2,1,0:T(2,128)S(1)}, u32[]{:S(2)}, u32[]{:S(2)}) async-start(f32[16,4,2,128]{3,2,1,0:T(2,128)} %stack.2), calls=%async_computation | async-start | bytes 131072 | tf_op jit(solution)/shard_map/all_to_all | solution.py:143
